TPU v7x, 128 devices: a whole 4x4x4 slice. The times are simulated.
128 devices in a mesh: dp: 4 (over y_hi, core), head: 4 (over x), ctx: 8 (over z, y_lo).
Axes of the slice: x: 4, y: 4 (y_hi: 2, y_lo: 2; y = y_hi * 2 + y_lo), z: 4, core: 2. Of those that a mesh axis runs over, the one named last changes fastest.
Arguments:
- video: bfloat16 [16, 64, 24576], P('dp', 'head', 'ctx'), parts along dimension 0, may hold values from -6 to 6
- cache: bfloat16 [8, 64, 24576], P('dp', 'head', 'ctx'), parts along dimension 0, may hold values from -6 to 6
- conv_weight: bfloat16 [3, 3, 288, 192], replicated, may hold values from -0.125 to 0.125
- conv_bias: float32 [192], replicated, may hold values from -3 to 3
- down_weight: bfloat16 [768, 192], replicated, may hold values from -0.21875 to 0.21875
- patch_weight: bfloat16 [768, 5120], P(None, ('head', 'ctx')), may hold values from -0.21875 to 0.21875
- step_index: int32 [4], P('dp'), parts along dimension 0, may hold values from 0 to 999
- mod_weight: bfloat16 [256, 10240], P(None, ('head', 'ctx')), may hold values from -1 to 1
- qkv_weight: bfloat16 [5120, 20, 3, 128], P('ctx', 'head'), may hold values from -0.078125 to 0.078125
Outputs:
- attended: bfloat16 [16384, 2560], P(('dp', 'ctx'), 'head'), parts along dimension 0
There are 4 independent parts, one for each index of `dp`. A program takes and returns all parts, laid end to end along the dimension named above; an argument that names none is the same for every part. Nothing has to cross between parts.
All inputs are finite; a program needn't handle non-finite values.
Results may differ from a plain program's by a relative error of at most 0.015.
The roundings to bfloat16 on the way count: a program that leaves them out, or rounds other values in their place, can miss the bound.
Values may be sent and summed in bfloat16 or wider, within the bound.
No kernel may reach another device: no remote copies, remote signals or barrier semaphores. Data moves between devices by JAX's collectives and lax.ppermute only.
A program may use at most 128 MiB of HBM per device.

v0:
```python
import jax
import jax.numpy as jnp
from jax import lax
from jax.sharding import PartitionSpec as P

D = 5120
HDIM = 128
FREQ = 256


def with_halo(cells, sides, width):
    for axis, dim in sides:
        count = lax.axis_size(axis)
        ends = count - 1
        head = lax.slice_in_dim(cells, 0, width, axis=dim)
        tail = lax.slice_in_dim(cells, cells.shape[dim] - width, cells.shape[dim], axis=dim)
        cells = jnp.concatenate(
            [
                lax.ppermute(tail, axis, [(i, (i + 1) % count) for i in range(ends)]),
                cells,
                lax.ppermute(head, axis, [((i + 1) % count, i) for i in range(ends)]),
            ],
            axis=dim,
        )
    return cells


def silu_act(value):
    return value * jax.nn.sigmoid(value)


def shards(
    video,
    cache,
    conv_weight,
    conv_bias,
    down_weight,
    patch_weight,
    step_index,
    mod_weight,
    qkv_weight,
):
    cin = conv_weight.shape[2] // 3
    cmid = conv_weight.shape[3]
    frame_count = video.shape[0]
    tile_rows = video.shape[1]
    tile_cols = video.shape[2] // cin
    frames = jnp.concatenate([cache, video], 0).reshape(frame_count + 2, tile_rows, tile_cols, cin)
    padded = with_halo(frames, (("head", 1), ("ctx", 2)), 1)
    total = jnp.zeros((frame_count, tile_rows, tile_cols, cmid), jnp.float32)
    for time_tap in range(3):
        for row_tap in range(3):
            slab = padded[time_tap : time_tap + frame_count, row_tap : row_tap + tile_rows]
            stacked = jnp.concatenate(
                [slab[:, :, col_tap : col_tap + tile_cols] for col_tap in range(3)], -1
            )
            total = total + jnp.einsum(
                "fyxc,cd->fyxd",
                stacked,
                conv_weight[time_tap, row_tap],
                preferred_element_type=jnp.float32,
            )
    hidden = silu_act(total + conv_bias).astype(jnp.bfloat16)
    stacked = (
        hidden.reshape(frame_count, tile_rows // 2, 2, tile_cols // 2, 2, cmid)
        .transpose(0, 1, 3, 2, 4, 5)
        .reshape(-1, 4 * cmid)
    )
    reduced = silu_act(jnp.dot(stacked, down_weight, preferred_element_type=jnp.float32)).astype(
        jnp.bfloat16
    )
    reduced = reduced.reshape(frame_count, tile_rows // 2, tile_cols // 2, cmid)
    patches = reduced.reshape(frame_count, tile_rows // 4, 2, tile_cols // 4, 2, cmid).transpose(
        0, 1, 3, 2, 4, 5
    )
    patches = patches.reshape(-1, 4 * cmid)
    half = FREQ // 2
    freqs = jnp.exp(-jnp.log(10000.0) * jnp.arange(half, dtype=jnp.float32) / half)
    angles = step_index[0].astype(jnp.float32) * freqs
    timing = jnp.concatenate([jnp.cos(angles), jnp.sin(angles)]).astype(jnp.bfloat16)
    mod_share = jnp.dot(timing[None, :], mod_weight, preferred_element_type=jnp.float32)[0]
    modulation = lax.all_gather(mod_share, ("head", "ctx"), axis=0, tiled=True)
    scale = modulation[:D]
    shift = modulation[D:]
    embedded = jnp.dot(
        patches,
        lax.all_gather(patch_weight, ("head", "ctx"), axis=1, tiled=True),
        preferred_element_type=jnp.float32,
    )
    inverse = lax.rsqrt(jnp.mean(embedded * embedded, -1, keepdims=True) + 1e-06)
    normed = (embedded * inverse * (1.0 + scale) + shift).astype(jnp.bfloat16)
    gathered = lax.all_gather(normed, "head", axis=0, tiled=True)
    group_rows = gathered.shape[0]
    heads_here = qkv_weight.shape[1]
    out_cols = heads_here * 3 * HDIM
    piece = lax.all_gather(qkv_weight, "ctx", axis=0, tiled=True)
    qkv = jnp.dot(
        gathered, piece.reshape(piece.shape[0], out_cols), preferred_element_type=jnp.float32
    )
    qkv = qkv.astype(jnp.bfloat16).reshape(group_rows, heads_here, 3, HDIM)
    query = qkv[:, :, 0]
    keys = qkv[:, :, 1]
    values = qkv[:, :, 2]
    inv_root = 1.0 / jnp.sqrt(jnp.float32(HDIM))
    best = jnp.full((heads_here, group_rows), -1e30, jnp.float32)
    key_piece = lax.all_gather(keys, "ctx", axis=0, tiled=True)
    value_piece = lax.all_gather(values, "ctx", axis=0, tiled=True)
    scores = (
        jnp.einsum("qhd,khd->hqk", query, key_piece, preferred_element_type=jnp.float32) * inv_root
    )
    new_best = jnp.maximum(best, jnp.max(scores, -1))
    probs = jnp.exp(scores - new_best[..., None])
    denom = jnp.sum(probs, -1)
    accum = jnp.einsum(
        "hqk,khd->hqd", probs.astype(jnp.bfloat16), value_piece, preferred_element_type=jnp.float32
    )
    best, denom, accum = (new_best, denom, accum)
    result = (accum / denom[..., None]).astype(jnp.bfloat16)
    return result.transpose(1, 0, 2).reshape(group_rows, heads_here * HDIM)


def solution(mesh):
    return jax.shard_map(
        shards,
        mesh=mesh,
        in_specs=(
            P("dp", "head", "ctx"),
            P("dp", "head", "ctx"),
            P(),
            P(),
            P(),
            P(None, ("head", "ctx")),
            P("dp"),
            P(None, ("head", "ctx")),
            P("ctx", "head", None, None),
        ),
        out_specs=P(("dp", "ctx"), "head"),
        check_vma=False,
    )
```

profile of v0, /device:TPU:1, one launch (start us, length us, event | category | flops | bytes accessed | tf_op | source)
XLA Modules:
  0.0 923.7 jit_solution(17581543572212077937)
XLA Ops:
  7.3 0.9 constant_dynamic-update-slice_fusion.1
  8.3 1.1 constant_dynamic-update-slice_fusion
  10.8 4.6 collective-permute-start
  15.3 1.3 collective-permute-start.1
  19.2 141.1 %all-reduce = f32[10240]{0:T(1024)S(1)} all-reduce(f32[10240]{0:T(1024)S(1)} %dynamic-update-slice), channel_id=1, replica_groups=mesh['dp'=4,'head'=4,'ctx'=8] {'head','ctx'}, use_global_device_ids=true, to_apply=%add | all-reduce | flops 10240 | bytes 81920
  164.3 1.3 collective-permute-start.2
  165.6 1.5 collective-permute-start.3
  167.6 1.4 collective-permute-done.2
  168.9 1.9 fusion.81
  170.8 1.3 collective-permute-done.3
  172.1 2.1 fusion.73
  174.2 0.9 fusion.13
  175.2 0.9 fusion.25
  176.9 0.9 fusion.43
  177.8 0.9 fusion.49
  181.5 2.6 multiply_convert_fusion
  187.7 8.9 all-gather.8.cloned.1.call-done
  196.7 5.9 multiply_reduce_fusion.1
  202.6 1.5 add_convert_fusion
  204.8 3.1 copy.17
  208.0 63.2 %all-gather.10.cloned.1.call-done = bf16[512,5120]{1,0:T(8,128)(2,1)} async-done(((bf16[128,5120]{1,0:T(8,128)(2,1)}), bf16[512,5120]{1,0:T(8,128)(2,1)}) %all-gather.10.cloned.1.call-update) | async-done | bytes 5242896 | tf_op jit(solution)/shard_map/all_gather | solution.py:92
  271.2 381.9 %all-gather.12.cloned.1.call-done = bf16[5120,5,3,128]{0,3,2,1:T(8,128)(2,1)} async-done(((bf16[640,5,3,128]{0,3,2,1:T(8,128)(2,1)}), bf16[5120,5,3,128]{0,3,2,1:T(8,128)(2,1)}) %all-gather.12.cloned.1.call-update) | async-done | bytes 19660816 | tf_op jit(solution)/shard_map/all_gather | solution.py:96
  653.1 17.7 %convolution_convert_fusion = bf16[512,1920]{1,0:T(8,128)(2,1)} fusion(bf16[512,5120]{1,0:T(8,128)(2,1)} %all-gather.10.cloned.1.call-done, bf16[5120,1920]{0,1:T(8,128)(2,1)} %bitcast.113), kind=kOutput, calls=%fused_computation.24 | convolution fusion | flops 10067312640 | bytes 26869760 | tf_op jit(solution)/shard_map/dot_general | solution.py:97
  670.8 2.7 copy.18
  673.5 1.0 fusion.115
  674.5 1.1 copy.33
  676.2 110.6 %all-gather.14.cloned.1.call-done = bf16[4096,5,1,128]{3,0,1,2:T(8,128)(2,1)} async-done(((bf16[512,5,1,128]{3,0,1,2:T(8,128)(2,1)}), bf16[4096,5,1,128]{3,0,1,2:T(8,128)(2,1)}) %all-gather.14.cloned.1.call-update) | async-done | bytes 5242896 | tf_op jit(solution)/shard_map/all_gather | solution.py:106
  786.8 19.0 %multiply_reduce_fusion = (f32[5,512]{1,0:T(8,128)S(1)}, f32[5,512,4096]{2,1,0:T(8,128)}) fusion(bf16[4096,5,1,128]{3,0,1,2:T(8,128)(2,1)} %all-gather.14.cloned.1.call-done, bf16[512,5,3,128]{0,3,2,1:T(8,128)(2,1)S(1)} %bitcast.108), kind=kOutput, calls=%fused_computation.1 | convolution fusion | flops 2705323520 | bytes 47851520 | tf_op jit(solution)/shard_map/qhd,khd->hqk/dot_general | solution.py:109
  805.8 17.3 %fusion = f32[5,512]{1,0:T(8,128)S(1)} fusion(f32[5,512,4096]{2,1,0:T(8,128)} %get-tuple-element.47, f32[5,512]{1,0:T(8,128)S(1)} %broadcast_maximum_fusion), kind=kLoop, calls=%fused_computation.2 | loop fusion | flops 31454720 | bytes 41963520 | tf_op jit(solution)/shard_map/reduce_sum | solution.py:113
  823.2 75.6 %all-gather.16.cloned.1.call-done = bf16[4096,5,1,128]{0,3,1,2:T(8,128)(2,1)} async-done(((bf16[512,5,1,128]{0,3,1,2:T(8,128)(2,1)}), bf16[4096,5,1,128]{0,3,1,2:T(8,128)(2,1)}) %all-gather.16.cloned.1.call-update) | async-done | bytes 5242896 | tf_op jit(solution)/shard_map/all_gather | solution.py:107
  898.7 17.3 %divide_convert_fusion = bf16[512,5,128]{0,2,1:T(8,128)(2,1)S(1)} fusion(bf16[4096,5,1,128]{0,3,1,2:T(8,128)(2,1)} %all-gather.16.cloned.1.call-done, f32[5,512,4096]{2,1,0:T(8,128)} %get-tuple-element.47, f32[5,512]{1,0:T(8,128)S(1)} %broadcast_maximum_fusion, f32[512,5]{0,1:T(8,128)S(1)} %bitcast.112), kind=kOutput, calls=%fused_computation.84 | convolution fusion | flops 2716467200 | bytes 47861760 | tf_op jit(solution)/shard_map/hqk,khd->hqd/dot_general | solution.py:114
  916.1 1.1 copy.22
  (62 shorter events, 16.2 us)
Async XLA Ops:
  6.5 180.0 %copy-start = (bf16[768,192]{0,1:T(8,128)(2,1)S(1)}, bf16[768,192]{0,1:T(8,128)(2,1)}, u32[]{:S(2)}) copy-start(bf16[768,192]{0,1:T(8,128)(2,1)} %param.13) | copy-start | bytes 884740
  6.5 10.8 %copy-start.7 = (u32[128]{0:T(128)S(1)}, u32[128]{0:T(128)}, u32[]{:S(2)}) copy-start(u32[128]{0:T(128)} %constant.27) | copy-start | bytes 1540
  6.5 12.2 %copy-start.4 = (bf16[256,320]{0,1:T(8,128)(2,1)S(1)}, bf16[256,320]{0,1:T(8,128)(2,1)}, u32[]{:S(2)}) copy-start(bf16[256,320]{0,1:T(8,128)(2,1)} %param.16) | copy-start | bytes 491524
  6.5 190.1 %all-gather.8.cloned.1.call-start = ((), (), s32[]{:S(2)}) async-start(), calls=%async_computation | async-start | bytes 8110080 | tf_op jit(solution)/shard_map/all_gather | solution.py:87
  7.3 264.0 %all-gather.10.cloned.1.call-start = ((), (), s32[]{:S(2)}) async-start(), calls=%async_computation.1 | async-start | bytes 6553600 | tf_op jit(solution)/shard_map/all_gather | solution.py:92
  8.3 152.2 %copy-start.3 = (bf16[4,16,3072]{2,1,0:T(8,128)(2,1)S(1)}, bf16[4,16,3072]{2,1,0:T(8,128)(2,1)}, u32[]{:S(2)}) copy-start(bf16[4,16,3072]{2,1,0:T(8,128)(2,1)} %param.9) | copy-start | bytes 1179652
  10.8 151.3 %collective-permute-start = (bf16[6,1,32,96]{3,2,1,0:T(8,128)(2,1)}, bf16[6,1,32,96]{3,2,1,0:T(8,128)(2,1)}, u32[]{:S(2)}, u32[]{:S(2)}) collective-permute-start(bf16[6,1,32,96]{3,2,1,0:T(8,128)(2,1)} %get-tuple-element.35), channel_id=1, source_target_pairs={{0,8},{8,16},{16,24},{1,9},{9,17},{17,25},{2,10},{10,18},{18,26},{... | collective-permute-start | bytes 110600 | tf_op jit(solution)/shard_map/ppermute | solution.py:19
  15.3 148.0 %collective-permute-start.1 = (bf16[6,1,32,96]{3,2,1,0:T(8,128)(2,1)}, bf16[6,1,32,96]{3,2,1,0:T(8,128)(2,1)}, u32[]{:S(2)}, u32[]{:S(2)}) collective-permute-start(bf16[6,1,32,96]{3,2,1,0:T(8,128)(2,1)} %get-tuple-element.34), channel_id=1, source_target_pairs={{8,0},{16,8},{24,16},{9,1},{17,9},{25,17},{10,2},{18,10},{26,18},{... | collective-permute-start | bytes 110600 | tf_op jit(solution)/shard_map/ppermute | solution.py:21
  164.3 4.6 collective-permute-start.2
  165.6 6.5 collective-permute-start.3
  170.8 3.4 copy-start.5
  180.5 0.9 copy-start.6
  202.6 2.2 copy-start.2
  204.1 449.0 %all-gather.12.cloned.1.call-start = ((), (), s32[]{:S(2)}) async-start(), calls=%async_computation.2 | async-start | bytes 22118400 | tf_op jit(solution)/shard_map/all_gather | solution.py:96
  207.9 578.8 %all-gather.14.cloned.1.call-start = ((), (), s32[]{:S(2)}) async-start(), calls=%async_computation.3 | async-start | bytes 5898240 | tf_op jit(solution)/shard_map/all_gather | solution.py:106
  675.6 223.2 %all-gather.16.cloned.1.call-start = ((), (), s32[]{:S(2)}) async-start(), calls=%async_computation.4 | async-start | bytes 5898240 | tf_op jit(solution)/shard_map/all_gather | solution.py:107
  898.7 18.4 %copy-start.1 = (bf16[768,192]{0,1:T(8,128)(2,1)S(1)}, bf16[768,192]{0,1:T(8,128)(2,1)}, u32[]{:S(2)}) copy-start(bf16[768,192]{0,1:T(8,128)(2,1)} %param.13) | copy-start | bytes 884740
Sparse Core Ops, SparseCore 0:
  9.0 187.6 all-gather.7
  204.2 66.9 all-gather.9
  272.9 380.1 all-gather.11
  675.7 111.0 all-gather.13
  788.3 110.4 all-gather.15
where the time goes:
time: 924 us
  waiting for transfers between devices  644 us (70%)
  blocking collectives  141 us (15%)
  matrix products  70.4 us (8%)
  other arithmetic  22.9 us (2%)
  local copies, waits for them, and re-layouts  21.4 us (2%)
  between operations  14.9 us (2%)
    all_gather x1, waiting for transfers between devices, shards(): piece = lax.all_gather(qkv_weight, 'ctx', axis=0, tiled=True)  382 us
    unnamed x1, blocking collectives  141 us
    all_gather x1, waiting for transfers between devices, shards(): key_piece = lax.all_gather(keys, 'ctx', axis=0, tiled=True)  111 us
    all_gather x1, waiting for transfers between devices, shards(): value_piece = lax.all_gather(values, 'ctx', axis=0, tiled=True)  75.6 us
    all_gather x1, waiting for transfers between devices, shards(): gathered = lax.all_gather(normed, 'head', axis=0, tiled=True)  63.2 us
    dot_general x1, matrix products, shards(): jnp.einsum('qhd,khd->hqk', query, key_piece, preferred_element_type=jnp.f...  19 us
  transfers between devices with their start and end apart: 9, of which 7 were waited for; matrix products, arithmetic and copies ran while one was open for 7% of the time, Pallas kernels for 0%

commit v1 on v0

--- a/solution.py
+++ b/solution.py
@@ -6,6 +6,17 @@
 D = 5120
 HDIM = 128
 FREQ = 256
+
+
+def pass_along(x, mesh_axis, along):
+    size = lax.axis_size(mesh_axis)
+    forward = [(i, (i + 1) % size) for i in range(size)]
+    parts = [x]
+    for far in range(1, size):
+        parts = [lax.ppermute(parts[0], mesh_axis, forward), *parts]
+    result = jnp.concatenate(parts, axis=along)
+    offset = (lax.axis_index(mesh_axis) + 1) * parts[-1].shape[along]
+    return jnp.roll(result, offset, axis=along)
 
 
 def with_halo(cells, sides, width):
@@ -89,7 +100,7 @@
     )
     inverse = lax.rsqrt(jnp.mean(embedded * embedded, -1, keepdims=True) + 1e-06)
     normed = (embedded * inverse * (1.0 + scale) + shift).astype(jnp.bfloat16)
-    gathered = lax.all_gather(normed, "head", axis=0, tiled=True)
+    gathered = pass_along(normed, "head", 0)
     group_rows = gathered.shape[0]
     heads_here = qkv_weight.shape[1]
     out_cols = heads_here * 3 * HDIM

time: 924 us -> 850 us (0.920)
  waiting for transfers between devices: 644 us -> 547 us
  local copies, waits for them, and re-layouts: 21.4 us -> 35.1 us
  starting transfers between devices: 8.77 us -> 19.2 us
    all_gather x1, waiting for transfers between devices: 382 us -> 282 us  [shards(): piece = lax.all_gather(qkv_weight, 'ctx', axis=0, tiled=True)]
    ppermute x0 -> x3, waiting for transfers between devices: none -> 67.1 us  [pass_along(): parts = [lax.ppermute(parts[0], mesh_axis, forward), *parts]]
    all_gather x1 -> x0, waiting for transfers between devices: 63.2 us -> none  [shards(): gathered = lax.all_gather(normed, 'head', axis=0, tiled=True)]
    unnamed x24 -> x34, local copies, waits for them, and re-layouts: 8.06 us -> 22.8 us
    ppermute x0 -> x3, starting transfers between devices: none -> 10.5 us  [pass_along(): parts = [lax.ppermute(parts[0], mesh_axis, forward), *parts]]
  transfers between devices with their start and end apart: 9 -> 11, of which waited for: 7 -> 9; matrix products, arithmetic and copies ran while one was open for 7% -> 10% of each run, Pallas kernels for 0% -> 0%
where the time goes in v1:
time: 850 us; the launch traced here: 849 us
  waiting for transfers between devices  547 us (64%)
  blocking collectives  138 us (16%)
  matrix products  70.4 us (8%)
  local copies, waits for them, and re-layouts  35.1 us (4%)
  other arithmetic  24.9 us (3%)
  starting transfers between devices  19.2 us (2%)
  between operations  14.8 us (2%)
    all_gather x1, waiting for transfers between devices, shards(): piece = lax.all_gather(qkv_weight, 'ctx', axis=0, tiled=True)  282 us
    unnamed x1, blocking collectives  138 us
    all_gather x1, waiting for transfers between devices, shards(): key_piece = lax.all_gather(keys, 'ctx', axis=0, tiled=True)  111 us
    all_gather x1, waiting for transfers between devices, shards(): value_piece = lax.all_gather(values, 'ctx', axis=0, tiled=True)  75.6 us
    ppermute x3, waiting for transfers between devices, pass_along(): parts = [lax.ppermute(parts[0], mesh_axis, forward), *parts]  67.1 us
    unnamed x34, local copies, waits for them, and re-layouts  22.8 us
    dot_general x1, matrix products, shards(): jnp.einsum('qhd,khd->hqk', query, key_piece, preferred_element_type=jnp.f...  19.1 us
    dot_general x1, matrix products, shards(): jnp.dot(gathered, piece.reshape(piece.shape[0], out_cols), preferred_elem...  17.7 us
  transfers between devices with their start and end apart: 11, of which 9 were waited for; matrix products, arithmetic and copies ran while one was open for 10% of the time, Pallas kernels for 0%

profile of v1, /device:TPU:1, one launch (start us, length us, event | category | flops | bytes accessed | tf_op | source)
XLA Modules:
  0.0 849.1 jit_solution(3823362946533361527)
XLA Ops:
  7.3 5.1 copy.17
  14.9 4.6 collective-permute-start
  19.5 1.3 collective-permute-start.1
  23.2 138.2 %all-reduce = f32[10240]{0:T(1024)S(1)} all-reduce(f32[10240]{0:T(1024)S(1)} %dynamic-update-slice), channel_id=1, replica_groups=mesh['dp'=4,'head'=4,'ctx'=8] {'head','ctx'}, use_global_device_ids=true, to_apply=%add | all-reduce | flops 10240 | bytes 81920
  165.4 1.3 collective-permute-start.2
  166.7 1.5 collective-permute-start.3
  168.7 1.3 collective-permute-done.2
  170.0 1.9 fusion.86
  171.9 1.3 collective-permute-done.3
  173.2 2.1 fusion.78
  182.6 2.6 multiply_convert_fusion
  188.8 7.1 all-gather.7.cloned.1.call-done
  195.9 5.9 multiply_reduce_fusion.1
  203.1 17.1 %collective-permute-done.4 = bf16[128,5120]{1,0:T(8,128)(2,1)S(1)} collective-permute-done((bf16[128,5120]{1,0:T(8,128)(2,1)S(1)}, bf16[128,5120]{1,0:T(8,128)(2,1)S(1)}, u32[]{:S(2)}, u32[]{:S(2)}) %collective-permute-start.4) | collective-permute-done | bytes 1310752 | tf_op jit(solution)/shard_map/ppermute | solution.py:16
  221.3 9.4 %collective-permute-start.5 = (bf16[128,5120]{1,0:T(8,128)(2,1)S(1)}, bf16[128,5120]{1,0:T(8,128)(2,1)}, u32[]{:S(2)}, u32[]{:S(2)}) collective-permute-start(bf16[128,5120]{1,0:T(8,128)(2,1)S(1)} %collective-permute-done.4), channel_id=1, source_target_pairs={{0,8},{8,16},{16,24},{24,0},{1,9},{9,17},{17,25},{25,1},{2,10},{10... | collective-permute-start | bytes 3932168 | tf_op jit(solution)/shard_map/ppermute | solution.py:16
  230.6 23.1 %collective-permute-done.5 = bf16[128,5120]{1,0:T(8,128)(2,1)} collective-permute-done((bf16[128,5120]{1,0:T(8,128)(2,1)S(1)}, bf16[128,5120]{1,0:T(8,128)(2,1)}, u32[]{:S(2)}, u32[]{:S(2)}) %collective-permute-start.5) | collective-permute-done | bytes 1310752 | tf_op jit(solution)/shard_map/ppermute | solution.py:16
  254.2 26.9 %collective-permute-done.6 = bf16[128,5120]{1,0:T(8,128)(2,1)} collective-permute-done((bf16[128,5120]{1,0:T(8,128)(2,1)}, bf16[128,5120]{1,0:T(8,128)(2,1)}, u32[]{:S(2)}, u32[]{:S(2)}) %collective-permute-start.6) | collective-permute-done | bytes 1310752 | tf_op jit(solution)/shard_map/ppermute | solution.py:16
  281.0 2.5 constant_dynamic-update-slice_fusion.16
  283.5 2.5 constant_dynamic-update-slice_fusion.15
  286.0 1.2 constant_dynamic-update-slice_fusion.14
  287.2 1.5 constant_dynamic-update-slice_fusion.13
  288.7 2.6 constant_dynamic-update-slice_fusion.12
  291.3 2.5 constant_dynamic-update-slice_fusion.11
  294.9 1.6 constant_dynamic-update-slice_fusion.9
  296.4 282.0 %all-gather.9.cloned.1.call-done = bf16[5120,5,3,128]{0,3,2,1:T(8,128)(2,1)} async-done(((bf16[640,5,3,128]{0,3,2,1:T(8,128)(2,1)}), bf16[5120,5,3,128]{0,3,2,1:T(8,128)(2,1)}) %all-gather.9.cloned.1.call-update) | async-done | bytes 19660816 | tf_op jit(solution)/shard_map/all_gather | solution.py:107
  578.5 17.7 %fusion.9 = bf16[512,1920]{1,0:T(8,128)(2,1)} fusion(bf16[5120,1920]{0,1:T(8,128)(2,1)} %bitcast.112, bf16[1024,5120]{1,0:T(8,128)(2,1)} %constant_dynamic-update-slice_fusion.9, s32[]{:T(128)S(6)} %select_n.14), kind=kOutput, calls=%fused_computation.26 | convolution fusion | flops 10067312640 | bytes 26869764 | tf_op jit(solution)/shard_map/dot_general | solution.py:108
  596.2 2.7 copy.18
  601.5 110.7 %all-gather.11.cloned.1.call-done = bf16[4096,5,1,128]{3,0,1,2:T(8,128)(2,1)} async-done(((bf16[512,5,1,128]{3,0,1,2:T(8,128)(2,1)}), bf16[4096,5,1,128]{3,0,1,2:T(8,128)(2,1)}) %all-gather.11.cloned.1.call-update) | async-done | bytes 5242896 | tf_op jit(solution)/shard_map/all_gather | solution.py:117
  712.2 19.1 %multiply_reduce_fusion = (f32[5,512]{1,0:T(8,128)S(1)}, f32[5,512,4096]{2,1,0:T(8,128)}) fusion(bf16[4096,5,1,128]{3,0,1,2:T(8,128)(2,1)} %all-gather.11.cloned.1.call-done, bf16[512,5,3,128]{0,3,2,1:T(8,128)(2,1)S(1)} %bitcast.107), kind=kOutput, calls=%fused_computation.1 | convolution fusion | flops 2705323520 | bytes 47851520 | tf_op jit(solution)/shard_map/qhd,khd->hqk/dot_general | solution.py:120
  731.3 17.3 %fusion = f32[5,512]{1,0:T(8,128)S(1)} fusion(f32[5,512,4096]{2,1,0:T(8,128)} %get-tuple-element.47, f32[5,512]{1,0:T(8,128)S(1)} %broadcast_maximum_fusion), kind=kLoop, calls=%fused_computation.2 | loop fusion | flops 31454720 | bytes 41963520 | tf_op jit(solution)/shard_map/reduce_sum | solution.py:124
  748.6 75.6 %all-gather.13.cloned.1.call-done = bf16[4096,5,1,128]{0,3,1,2:T(8,128)(2,1)} async-done(((bf16[512,5,1,128]{0,3,1,2:T(8,128)(2,1)}), bf16[4096,5,1,128]{0,3,1,2:T(8,128)(2,1)}) %all-gather.13.cloned.1.call-update) | async-done | bytes 5242896 | tf_op jit(solution)/shard_map/all_gather | solution.py:118
  824.2 17.3 %divide_convert_fusion = bf16[512,5,128]{0,2,1:T(8,128)(2,1)S(1)} fusion(bf16[4096,5,1,128]{0,3,1,2:T(8,128)(2,1)} %all-gather.13.cloned.1.call-done, f32[5,512,4096]{2,1,0:T(8,128)} %get-tuple-element.47, f32[5,512]{1,0:T(8,128)S(1)} %broadcast_maximum_fusion, f32[512,5]{0,1:T(8,128)S(1)} %bitcast.111), kind=kOutput, calls=%fused_computation.86 | convolution fusion | flops 2716467200 | bytes 47861760 | tf_op jit(solution)/shard_map/hqk,khd->hqd/dot_general | solution.py:125
  (77 shorter events, 26.9 us)
Async XLA Ops:
  6.5 181.1 %copy-start = (bf16[768,192]{0,1:T(8,128)(2,1)S(1)}, bf16[768,192]{0,1:T(8,128)(2,1)}, u32[]{:S(2)}) copy-start(bf16[768,192]{0,1:T(8,128)(2,1)} %param.13) | copy-start | bytes 884740
  6.5 189.4 %all-gather.7.cloned.1.call-start = ((), (), s32[]{:S(2)}) async-start(), calls=%async_computation | async-start | bytes 8110080 | tf_op jit(solution)/shard_map/all_gather | solution.py:98
  7.3 571.2 %all-gather.9.cloned.1.call-start = ((), (), s32[]{:S(2)}) async-start(), calls=%async_computation.1 | async-start | bytes 22118400 | tf_op jit(solution)/shard_map/all_gather | solution.py:107
  12.4 0.9 copy-start.5
  12.4 1.1 copy-start.4
  12.4 9.1 %copy-start.9 = (u32[128]{0:T(128)S(1)}, u32[128]{0:T(128)}, u32[]{:S(2)}) copy-start(u32[128]{0:T(128)} %constant.58) | copy-start | bytes 1540
  12.4 10.4 %copy-start.6 = (bf16[256,320]{0,1:T(8,128)(2,1)S(1)}, bf16[256,320]{0,1:T(8,128)(2,1)}, u32[]{:S(2)}) copy-start(bf16[256,320]{0,1:T(8,128)(2,1)} %param.16) | copy-start | bytes 491524
  12.4 699.8 %all-gather.11.cloned.1.call-start = ((), (), s32[]{:S(2)}) async-start(), calls=%async_computation.2 | async-start | bytes 5898240 | tf_op jit(solution)/shard_map/all_gather | solution.py:117
  14.9 148.2 %collective-permute-start = (bf16[6,1,32,96]{3,2,1,0:T(8,128)(2,1)}, bf16[6,1,32,96]{3,2,1,0:T(8,128)(2,1)}, u32[]{:S(2)}, u32[]{:S(2)}) collective-permute-start(bf16[6,1,32,96]{3,2,1,0:T(8,128)(2,1)} %get-tuple-element.35), channel_id=1, source_target_pairs={{0,8},{8,16},{16,24},{1,9},{9,17},{17,25},{2,10},{10,18},{18,26},{... | collective-permute-start | bytes 110600 | tf_op jit(solution)/shard_map/ppermute | solution.py:30
  19.5 145.0 %collective-permute-start.1 = (bf16[6,1,32,96]{3,2,1,0:T(8,128)(2,1)}, bf16[6,1,32,96]{3,2,1,0:T(8,128)(2,1)}, u32[]{:S(2)}, u32[]{:S(2)}) collective-permute-start(bf16[6,1,32,96]{3,2,1,0:T(8,128)(2,1)} %get-tuple-element.34), channel_id=1, source_target_pairs={{8,0},{16,8},{24,16},{9,1},{17,9},{25,17},{10,2},{18,10},{26,18},{... | collective-permute-start | bytes 110600 | tf_op jit(solution)/shard_map/ppermute | solution.py:32
  165.4 4.6 collective-permute-start.2
  166.7 6.5 collective-permute-start.3
  171.9 3.5 copy-start.7
  181.7 0.9 copy-start.8
  202.3 17.9 %collective-permute-start.4 = (bf16[128,5120]{1,0:T(8,128)(2,1)S(1)}, bf16[128,5120]{1,0:T(8,128)(2,1)S(1)}, u32[]{:S(2)}, u32[]{:S(2)}) collective-permute-start(bf16[128,5120]{1,0:T(8,128)(2,1)S(1)} %add_convert_fusion), channel_id=1, source_target_pairs={{0,8},{8,16},{16,24},{24,0},{1,9},{9,17},{17,25},{25,1},{2,10},{10... | collective-permute-start | bytes 3932168 | tf_op jit(solution)/shard_map/ppermute | solution.py:16
  220.2 1.1 copy-start.2
  221.3 32.5 %collective-permute-start.5 = (bf16[128,5120]{1,0:T(8,128)(2,1)S(1)}, bf16[128,5120]{1,0:T(8,128)(2,1)}, u32[]{:S(2)}, u32[]{:S(2)}) collective-permute-start(bf16[128,5120]{1,0:T(8,128)(2,1)S(1)} %collective-permute-done.4), channel_id=1, source_target_pairs={{0,8},{8,16},{16,24},{24,0},{1,9},{9,17},{17,25},{25,1},{2,10},{10... | collective-permute-start | bytes 3932168 | tf_op jit(solution)/shard_map/ppermute | solution.py:16
  253.8 27.2 %collective-permute-start.6 = (bf16[128,5120]{1,0:T(8,128)(2,1)}, bf16[128,5120]{1,0:T(8,128)(2,1)}, u32[]{:S(2)}, u32[]{:S(2)}) collective-permute-start(bf16[128,5120]{1,0:T(8,128)(2,1)} %collective-permute-done.5), channel_id=1, source_target_pairs={{0,8},{8,16},{16,24},{24,0},{1,9},{9,17},{17,25},{25,1},{2,10},{10... | collective-permute-start | bytes 3932168 | tf_op jit(solution)/shard_map/ppermute | solution.py:16
  254.2 31.9 %copy-start.3 = (bf16[128,5120]{1,0:T(8,128)(2,1)S(1)}, bf16[128,5120]{1,0:T(8,128)(2,1)}, u32[]{:S(2)}) copy-start(bf16[128,5120]{1,0:T(8,128)(2,1)} %copy-done.2) | copy-start | bytes 3932164
  600.9 223.3 %all-gather.13.cloned.1.call-start = ((), (), s32[]{:S(2)}) async-start(), calls=%async_computation.3 | async-start | bytes 5898240 | tf_op jit(solution)/shard_map/all_gather | solution.py:118
  824.2 18.4 %copy-start.1 = (bf16[768,192]{0,1:T(8,128)(2,1)S(1)}, bf16[768,192]{0,1:T(8,128)(2,1)}, u32[]{:S(2)}) copy-start(bf16[768,192]{0,1:T(8,128)(2,1)} %param.13) | copy-start | bytes 884740
Sparse Core Ops, SparseCore 0:
  9.0 186.8 all-gather.6
  197.6 380.8 all-gather.8
  601.1 111.1 all-gather.10
  713.8 110.4 all-gather.12
